TPU v7x, 512 devices: a whole 4x4x16 slice. The times are simulated.
512 devices in a mesh: pos: 64 (over z, y), mode: 8 (over x, core).
Axes of the slice: x: 4, y: 4, z: 16, core: 2. Of those that a mesh axis runs over, the one named last changes fastest.
Arguments:
- object_field: float32 [2, 8192, 512], P(None, 'pos'), may hold values from -6 to 6
- probe: float32 [2, 8, 256, 256], P(None, 'mode'), may hold values from -3 to 3
- measured: float32 [192, 256, 256], P('pos'), may hold values from 0 to 16
- row_offsets: int32 [192], P('pos'), may hold values from 0 to 127
- col_offsets: int32 [192], P('pos'), may hold values from 0 to 256
- tile_counts: int32 [64], P('pos'), may hold values from 1 to 3, 96 in all
Outputs:
- updated_object: float32 [2, 8192, 512], P(None, ('pos', 'mode'))
Inputs may be any that keep to these rules, and one draw needn't show every extreme that they name: Slots 0 to tile_counts[t] - 1 of tile t hold scan positions, the others are empty; the counts sum to 96 and the largest equals 3.
All inputs are finite; a program needn't handle non-finite values. No bound on the sum of `tile_counts` on one device may be relied on, other than what follows from the above.
Results may differ from a plain program's by a relative error of at most 0.0016.
Values sent between devices are 32-bit elements; how exact they have to be, the bound alone decides.
No kernel may reach another device: no remote copies, remote signals or barrier semaphores. Data moves between devices by JAX's collectives and lax.ppermute only.
A program may use at most 64 MiB of HBM per device.

v0:
```python
import math
import jax
import jax.numpy as jnp
from jax import lax
from jax.sharding import PartitionSpec as P


def extended_2(array, sides, width):
    for axis, dim in sides:
        size, length = (lax.axis_size(axis), array.shape[dim])
        up = [(i, (i + 1) % size) for i in range(size - 1)]
        down = [(j, i) for i, j in up]
        last = lax.slice_in_dim(array, length - width, length, axis=dim)
        first = lax.slice_in_dim(array, 0, width, axis=dim)
        before = lax.ppermute(last, axis, up)
        after = lax.ppermute(first, axis, down)
        array = jnp.concatenate([before, array, after], axis=dim)
    return array


def dft_tables(pattern):
    counter = jnp.arange(pattern, dtype=jnp.int32)
    phases = counter[:, None] * counter[None, :] % pattern
    angles = phases.astype(jnp.float32) * (2.0 * math.pi / pattern)
    factor = 1.0 / math.sqrt(pattern)
    return (
        (jnp.cos(angles) * factor).astype(jnp.bfloat16),
        (-jnp.sin(angles) * factor).astype(jnp.bfloat16),
    )


def left_product(table, stacked):
    return jnp.einsum("ua,kab->kub", table, stacked, preferred_element_type=jnp.float32)


def right_product(stacked, table):
    return jnp.einsum("kub,bv->kuv", stacked, table, preferred_element_type=jnp.float32)


def local(object_field, probe, measured, row_offsets, col_offsets, tile_counts):
    rows_tile = object_field.shape[1]
    columns = object_field.shape[2]
    pattern = probe.shape[2]
    slot_count = measured.shape[0]
    mode_count = lax.axis_size("mode")
    my_mode = lax.axis_index("mode")
    share_rows = rows_tile // mode_count
    real_table, imag_table = dft_tables(pattern)
    anchor = jnp.zeros((), jnp.int32)
    extended = extended_2(object_field, (("pos", 1),), rows_tile)
    probe_re = probe[0]
    probe_im = probe[1]
    top_rows = rows_tile + row_offsets - pattern // 2

    def forward(position):
        window = lax.dynamic_slice(
            extended, (anchor, top_rows[position], col_offsets[position]), (2, pattern, pattern)
        )
        exit_re = (probe_re * window[0] - probe_im * window[1]).astype(jnp.bfloat16)
        exit_im = (probe_re * window[1] + probe_im * window[0]).astype(jnp.bfloat16)
        half_re = (left_product(real_table, exit_re) - left_product(imag_table, exit_im)).astype(
            jnp.bfloat16
        )
        half_im = (left_product(real_table, exit_im) + left_product(imag_table, exit_re)).astype(
            jnp.bfloat16
        )
        wave_re = right_product(half_re, real_table) - right_product(half_im, imag_table)
        wave_im = right_product(half_re, imag_table) + right_product(half_im, real_table)
        return (exit_re, exit_im, wave_re, wave_im)

    exit_re, exit_im, wave_re, wave_im = lax.map(forward, jnp.arange(slot_count, dtype=jnp.int32))
    power_sum = jnp.sum(wave_re * wave_re + wave_im * wave_im, axis=1)
    model_power = lax.psum(power_sum, "mode")
    scaling = jnp.sqrt(measured) / jnp.maximum(jnp.sqrt(model_power), 1.0)
    probe_power = jnp.sum(probe_re * probe_re + probe_im * probe_im, axis=0)
    live_count = tile_counts[0]

    def backward(position, buffer):
        fixed_re = (scaling[position] * wave_re[position]).astype(jnp.bfloat16)
        fixed_im = (scaling[position] * wave_im[position]).astype(jnp.bfloat16)
        back_re = (left_product(real_table, fixed_re) + left_product(imag_table, fixed_im)).astype(
            jnp.bfloat16
        )
        back_im = (left_product(real_table, fixed_im) - left_product(imag_table, fixed_re)).astype(
            jnp.bfloat16
        )
        delta_re = (
            right_product(back_re, real_table)
            + right_product(back_im, imag_table)
            - exit_re[position].astype(jnp.float32)
        )
        delta_im = (
            right_product(back_im, real_table)
            - right_product(back_re, imag_table)
            - exit_im[position].astype(jnp.float32)
        )
        numer_re = jnp.sum(probe_re * delta_re + probe_im * delta_im, axis=0)
        numer_im = jnp.sum(probe_re * delta_im - probe_im * delta_re, axis=0)
        contrib = jnp.stack([numer_re, numer_im, probe_power])
        contrib = jnp.where(position < live_count, contrib, jnp.zeros_like(contrib))
        corner = (anchor, top_rows[position], col_offsets[position])
        current = lax.dynamic_slice(buffer, corner, (3, pattern, pattern))
        return lax.dynamic_update_slice(buffer, current + contrib, corner)

    buffer = lax.fori_loop(
        0, slot_count, backward, jnp.zeros((3, 3 * rows_tile, columns), jnp.float32)
    )
    outside = jnp.concatenate([buffer[:, :rows_tile], buffer[:, 2 * rows_tile :]], axis=1)
    framed_sum = extended_2(outside, (("pos", 1),), rows_tile)
    tile_sum = (
        buffer[:, rows_tile : 2 * rows_tile]
        + framed_sum[:, :rows_tile]
        + framed_sum[:, 3 * rows_tile :]
    )
    update_sum = lax.psum_scatter(tile_sum, "mode", scatter_dimension=1, tiled=True)
    own_rows = lax.dynamic_slice_in_dim(object_field, my_mode * share_rows, share_rows, 1)
    return own_rows + update_sum[:2] / (update_sum[2] + 1.0)


def solution(mesh):
    in_specs = (
        P(None, "pos", None),
        P(None, "mode", None, None),
        P("pos", None, None),
        P("pos"),
        P("pos"),
        P("pos"),
    )
    out_specs = P(None, ("pos", "mode"), None)
    return jax.shard_map(local, mesh=mesh, in_specs=in_specs, out_specs=out_specs, check_vma=False)
```

profile of v0, /device:TPU:8, one launch (start us, length us, event | category | flops | bytes accessed | tf_op | source)
XLA Modules:
  0.0 350.2 jit_solution(2317298614045170838)
XLA Ops:
  6.5 3.6 %collective-permute-start = (f32[2,128,512]{2,1,0:T(8,128)}, f32[2,128,512]{2,1,0:T(8,128)S(1)}, u32[]{:S(2)}, u32[]{:S(2)}) collective-permute-start(f32[2,128,512]{2,1,0:T(8,128)} %param.10), channel_id=1, source_target_pairs={{0,8},{8,16},{16,24},{24,32},{32,40},{40,48},{48,56},{56,64},{64,7... | collective-permute-start | bytes 1572872 | tf_op jit(solution)/shard_map/ppermute | solution.py:15
  10.2 5.6 %collective-permute-start.1 = (f32[2,128,512]{2,1,0:T(8,128)}, f32[2,128,512]{2,1,0:T(8,128)S(1)}, u32[]{:S(2)}, u32[]{:S(2)}) collective-permute-start(f32[2,128,512]{2,1,0:T(8,128)} %param.10), channel_id=1, source_target_pairs={{8,0},{16,8},{24,16},{32,24},{40,32},{48,40},{56,48},{64,56},{72,6... | collective-permute-start | bytes 1572872 | tf_op jit(solution)/shard_map/ppermute | solution.py:16
  15.8 1.9 add_bitcast_fusion
  17.7 4.8 %collective-permute-done = f32[2,128,512]{2,1,0:T(8,128)S(1)} collective-permute-done((f32[2,128,512]{2,1,0:T(8,128)}, f32[2,128,512]{2,1,0:T(8,128)S(1)}, u32[]{:S(2)}, u32[]{:S(2)}) %collective-permute-start) | collective-permute-done | bytes 524320 | tf_op jit(solution)/shard_map/ppermute | solution.py:15
  22.4 3.2 collective-permute-done.1
  26.8 60.4 %while.33 = (s32[]{:T(128)}, bf16[3,1,256,256]{3,2,1,0:T(8,128)(2,1)}, bf16[3,1,256,256]{3,2,1,0:T(8,128)(2,1)}, f32[3,1,256,256]{3,2,1,0:T(8,128)}, f32[3,1,256...) while((s32[]{:T(128)}, ...), condition=%wide.region_1.2_spmd.clone.clone, body=%wide.region_0.1_spmd.clone.clone.sunk | while | flops 278003712 | bytes 5506879 | solution.py:71
  34.4 2.0 bitcast_dynamic-update-slice_fusion.3
  42.1 1.9 fusion.201
  45.1 1.9 fusion.199
  54.5 1.9 bitcast_dynamic-update-slice_fusion.3
  62.2 1.9 fusion.201
  65.2 1.9 fusion.199
  74.7 2.0 bitcast_dynamic-update-slice_fusion.3
  85.3 1.9 fusion.199
  87.2 2.5 fusion.136
  89.9 83.1 %all-reduce.2.cloned.1.call-done = f32[3,256,256]{2,1,0:T(8,128)} async-done(((f32[3,256,256]{2,1,0:T(8,128)}), f32[3,256,256]{2,1,0:T(8,128)}) %all-reduce.2.cloned.1.call-update) | async-done | bytes 786448 | tf_op jit(solution)/shard_map/psum | solution.py:73
  173.0 2.5 maximum_divide_fusion
  175.8 99.1 %while.34 = (s32[]{:T(128)}, f32[3,384,512]{2,1,0:T(8,128)S(1)}, s32[3]{0:T(128)S(1)}, s32[3]{0:T(128)S(1)}, s32[]{:T(128)}, /*index=5*/f32[1,256,256]{2,1,0:T(8...) while((s32[]{:T(128)}, f32[3,384,512]{2,1,0:T(8,128)S(1)}, ...), condition=%wide.region_4.5_spmd.clone.clone, body=%wide.region_3.4_spmd.clone.clone.sunk | while | flops 279183360 | bytes 10223899 | solution.py:105
  182.7 2.1 fusion.216
  185.9 3.1 fusion.218
  196.4 13.6 %dynamic_update_slice.42 = f32[3,384,512]{2,1,0:T(8,128)S(1)} dynamic-update-slice(f32[3,384,512]{2,1,0:T(8,128)S(1)} %get-tuple-element.786, f32[3,256,256]{2,1,0:T(8,128)S(1)} %fusion.219, s32[]{:T(128)} %constant.88.clone.1..sunk.1, s32[]{:T(128)S(6)} %select_n.210, s32[]{:T(128)S(6)} %select_n.211) | dynamic-update-slice | bytes 1572868 | tf_op jit(solution)/shard_map/while/body/eval_jaxpr/dynamic_update_slice | solution.py:103
  216.9 2.1 fusion.216
  220.1 3.1 fusion.218
  230.7 11.0 %dynamic_update_slice.42 = f32[3,384,512]{2,1,0:T(8,128)S(1)} dynamic-update-slice(f32[3,384,512]{2,1,0:T(8,128)S(1)} %get-tuple-element.786, f32[3,256,256]{2,1,0:T(8,128)S(1)} %fusion.219, s32[]{:T(128)} %constant.88.clone.1..sunk.1, s32[]{:T(128)S(6)} %select_n.210, s32[]{:T(128)S(6)} %select_n.211) | dynamic-update-slice | bytes 1572868 | tf_op jit(solution)/shard_map/while/body/eval_jaxpr/dynamic_update_slice | solution.py:103
  248.6 2.1 fusion.216
  251.8 3.1 fusion.218
  262.4 12.6 %dynamic_update_slice.42 = f32[3,384,512]{2,1,0:T(8,128)S(1)} dynamic-update-slice(f32[3,384,512]{2,1,0:T(8,128)S(1)} %get-tuple-element.786, f32[3,256,256]{2,1,0:T(8,128)S(1)} %fusion.219, s32[]{:T(128)} %constant.88.clone.1..sunk.1, s32[]{:T(128)S(6)} %select_n.210, s32[]{:T(128)S(6)} %select_n.211) | dynamic-update-slice | bytes 1572868 | tf_op jit(solution)/shard_map/while/body/eval_jaxpr/dynamic_update_slice | solution.py:103
  275.1 1.9 collective-permute-start.2
  277.1 4.0 %collective-permute-start.3 = (f32[3,128,512]{2,1,0:T(8,128)S(1)}, f32[3,128,512]{2,1,0:T(8,128)S(1)}, u32[]{:S(2)}, u32[]{:S(2)}) collective-permute-start(f32[3,128,512]{2,1,0:T(8,128)S(1)} %get-tuple-element.551), channel_id=1, source_target_pairs={{8,0},{16,8},{24,16},{32,24},{40,32},{48,40},{56,48},{64,56},{72,6... | collective-permute-start | bytes 2359304 | tf_op jit(solution)/shard_map/ppermute | solution.py:16
  281.0 13.6 %collective-permute-done.2 = f32[3,128,512]{2,1,0:T(8,128)S(1)} collective-permute-done((f32[3,128,512]{2,1,0:T(8,128)S(1)}, f32[3,128,512]{2,1,0:T(8,128)S(1)}, u32[]{:S(2)}, u32[]{:S(2)}) %collective-permute-start.2) | collective-permute-done | bytes 786464 | tf_op jit(solution)/shard_map/ppermute | solution.py:15
  294.6 3.6 %collective-permute-done.3 = f32[3,128,512]{2,1,0:T(8,128)S(1)} collective-permute-done((f32[3,128,512]{2,1,0:T(8,128)S(1)}, f32[3,128,512]{2,1,0:T(8,128)S(1)}, u32[]{:S(2)}, u32[]{:S(2)}) %collective-permute-start.3) | collective-permute-done | bytes 786464 | tf_op jit(solution)/shard_map/ppermute | solution.py:16
  299.4 41.7 %reduce-scatter.2.cloned.1.call-done = f32[3,16,512]{2,1,0:T(8,128)} async-done(((f32[3,128,512]{2,1,0:T(8,128)}), f32[3,16,512]{2,1,0:T(8,128)}) %reduce-scatter.2.cloned.1.call-update) | async-done | bytes 98320 | tf_op jit(solution)/shard_map/reduce_scatter | solution.py:115
  (79 shorter events, 65.2 us)
Async XLA Ops:
  6.5 20.3 %copy-start.1 = (s32[3]{0:T(128)S(1)}, s32[3]{0:T(128)}, u32[]{:S(2)}) copy-start(s32[3]{0:T(128)} %param.13) | copy-start | bytes 40
  6.5 20.3 %copy-start.2 = (s32[3]{0:T(128)S(1)}, s32[3]{0:T(128)}, u32[]{:S(2)}) copy-start(s32[3]{0:T(128)} %param.14) | copy-start | bytes 40
  6.5 166.5 %all-reduce.2.cloned.1.call-start = ((), (), s32[]{:S(2)}) async-start(), calls=%async_computation.1 | async-start | bytes 1572864 | tf_op jit(solution)/shard_map/psum | solution.py:73
  6.5 15.9 %collective-permute-start = (f32[2,128,512]{2,1,0:T(8,128)}, f32[2,128,512]{2,1,0:T(8,128)S(1)}, u32[]{:S(2)}, u32[]{:S(2)}) collective-permute-start(f32[2,128,512]{2,1,0:T(8,128)} %param.10), channel_id=1, source_target_pairs={{0,8},{8,16},{16,24},{24,32},{32,40},{40,48},{48,56},{56,64},{64,7... | collective-permute-start | bytes 1572872 | tf_op jit(solution)/shard_map/ppermute | solution.py:15
  10.2 15.5 %collective-permute-start.1 = (f32[2,128,512]{2,1,0:T(8,128)}, f32[2,128,512]{2,1,0:T(8,128)S(1)}, u32[]{:S(2)}, u32[]{:S(2)}) collective-permute-start(f32[2,128,512]{2,1,0:T(8,128)} %param.10), channel_id=1, source_target_pairs={{8,0},{16,8},{24,16},{32,24},{40,32},{48,40},{56,48},{64,56},{72,6... | collective-permute-start | bytes 1572872 | tf_op jit(solution)/shard_map/ppermute | solution.py:16
  87.2 85.8 %copy-start = (f32[3,256,256]{2,1,0:T(8,128)S(1)}, f32[3,256,256]{2,1,0:T(8,128)}, u32[]{:S(2)}) copy-start(f32[3,256,256]{2,1,0:T(8,128)} %param.12) | copy-start | bytes 2359300
  89.7 251.4 %reduce-scatter.2.cloned.1.call-start = ((), (), s32[]{:S(2)}) async-start(), calls=%async_computation.2 | async-start | bytes 884736 | tf_op jit(solution)/shard_map/reduce_scatter | solution.py:115
  275.1 19.5 %collective-permute-start.2 = (f32[3,128,512]{2,1,0:T(8,128)S(1)}, f32[3,128,512]{2,1,0:T(8,128)S(1)}, u32[]{:S(2)}, u32[]{:S(2)}) collective-permute-start(f32[3,128,512]{2,1,0:T(8,128)S(1)} %get-tuple-element.550), channel_id=1, source_target_pairs={{0,8},{8,16},{16,24},{24,32},{32,40},{40,48},{48,56},{56,64},{64,7... | collective-permute-start | bytes 2359304 | tf_op jit(solution)/shard_map/ppermute | solution.py:15
  277.1 21.1 %collective-permute-start.3 = (f32[3,128,512]{2,1,0:T(8,128)S(1)}, f32[3,128,512]{2,1,0:T(8,128)S(1)}, u32[]{:S(2)}, u32[]{:S(2)}) collective-permute-start(f32[3,128,512]{2,1,0:T(8,128)S(1)} %get-tuple-element.551), channel_id=1, source_target_pairs={{8,0},{16,8},{24,16},{32,24},{40,32},{48,40},{56,48},{64,56},{72,6... | collective-permute-start | bytes 2359304 | tf_op jit(solution)/shard_map/ppermute | solution.py:16
Sparse Core Ops, SparseCore 0:
  89.8 83.1 all-reduce.1
  299.5 41.5 reduce-scatter.1
where the time goes:
time: 351 us; the launch traced here: 350 us
  waiting for transfers between devices  150 us (43%)
  matrix products  67.6 us (19%)
  local copies, waits for them, and re-layouts  47.3 us (13%)
  loops' own time  31.8 us (9%)
  other arithmetic  24.8 us (7%)
  starting transfers between devices  15.3 us (4%)
  between operations  13.5 us (4%)
    psum x1, waiting for transfers between devices, local(): model_power = lax.psum(power_sum, 'mode')  83.1 us
    reduce_scatter x1, waiting for transfers between devices, local(): lax.psum_scatter(tile_sum, 'mode', scatter_dimension=1, tiled=True)  41.7 us
    dot_general x24, matrix products, right_product(): jnp.einsum('kub,bv->kuv', stacked, table, preferred_element_type=jnp.floa...  40.3 us
    dynamic_update_slice x3, local copies, waits for them, and re-layouts, backward(): return lax.dynamic_update_slice(buffer, current + contrib, corner)  37.2 us
    dot_general x24, matrix products, left_product(): jnp.einsum('ua,kab->kub', table, stacked, preferred_element_type=jnp.floa...  27.3 us
    ppermute x2, waiting for transfers between devices, extended_2(): before = lax.ppermute(last, axis, up)  18.4 us
    another operation x1, loops' own time, local(): lax.map(forward, jnp.arange(slot_count, dtype=jnp.int32))  17.2 us
    another operation x1, loops' own time, local(): lax.fori_loop(0, slot_count, backward, jnp.zeros((3, 3 * rows_tile, colum...  14.6 us
  transfers between devices with their start and end apart: 6, of which 6 were waited for; matrix products, arithmetic and copies ran while one was open for 1% of the time, Pallas kernels for 0%

commit v1 on v0

--- a/solution.py
+++ b/solution.py
@@ -70,7 +70,8 @@
 
     exit_re, exit_im, wave_re, wave_im = lax.map(forward, jnp.arange(slot_count, dtype=jnp.int32))
     power_sum = jnp.sum(wave_re * wave_re + wave_im * wave_im, axis=1)
-    model_power = lax.psum(power_sum, "mode")
+    parts = lax.all_gather(power_sum, "mode")
+    model_power = jnp.sum(parts, axis=0)
     scaling = jnp.sqrt(measured) / jnp.maximum(jnp.sqrt(model_power), 1.0)
     probe_power = jnp.sum(probe_re * probe_re + probe_im * probe_im, axis=0)
     live_count = tile_counts[0]

time: 351 us -> 323 us (0.920)
  waiting for transfers between devices: 150 us -> 122 us
    psum x1 -> x0, waiting for transfers between devices: 83.1 us -> none  [local(): model_power = lax.psum(power_sum, 'mode')]
    all_gather x0 -> x1, waiting for transfers between devices: none -> 54.6 us  [local(): parts = lax.all_gather(power_sum, 'mode')]
where the time goes in v1:
time: 323 us; the launch traced here: 322 us
  waiting for transfers between devices  122 us (38%)
  matrix products  67.6 us (21%)
  local copies, waits for them, and re-layouts  46.7 us (14%)
  loops' own time  29.6 us (9%)
  other arithmetic  27 us (8%)
  starting transfers between devices  15.3 us (5%)
  between operations  13.5 us (4%)
    all_gather x1, waiting for transfers between devices, local(): parts = lax.all_gather(power_sum, 'mode')  54.6 us
    dot_general x24, matrix products, right_product(): jnp.einsum('kub,bv->kuv', stacked, table, preferred_element_type=jnp.floa...  40.3 us
    reduce_scatter x1, waiting for transfers between devices, local(): lax.psum_scatter(tile_sum, 'mode', scatter_dimension=1, tiled=True)  39.9 us
    dynamic_update_slice x3, local copies, waits for them, and re-layouts, backward(): return lax.dynamic_update_slice(buffer, current + contrib, corner)  37.2 us
    dot_general x24, matrix products, left_product(): jnp.einsum('ua,kab->kub', table, stacked, preferred_element_type=jnp.floa...  27.3 us
    ppermute x2, waiting for transfers between devices, extended_2(): before = lax.ppermute(last, axis, up)  20.5 us
    another operation x1, loops' own time, local(): lax.map(forward, jnp.arange(slot_count, dtype=jnp.int32))  17.3 us
    another operation x1, loops' own time, local(): lax.fori_loop(0, slot_count, backward, jnp.zeros((3, 3 * rows_tile, colum...  12.3 us
  transfers between devices with their start and end apart: 6, of which 6 were waited for; matrix products, arithmetic and copies ran while one was open for 1% of the time, Pallas kernels for 0%

profile of v1, /device:TPU:8, one launch (start us, length us, event | category | flops | bytes accessed | tf_op | source)
XLA Modules:
  0.0 321.9 jit_solution(16533029531524323770)
XLA Ops:
  6.5 3.6 %collective-permute-start = (f32[2,128,512]{2,1,0:T(8,128)}, f32[2,128,512]{2,1,0:T(8,128)S(1)}, u32[]{:S(2)}, u32[]{:S(2)}) collective-permute-start(f32[2,128,512]{2,1,0:T(8,128)} %param.10), channel_id=1, source_target_pairs={{0,8},{8,16},{16,24},{24,32},{32,40},{40,48},{48,56},{56,64},{64,7... | collective-permute-start | bytes 1572872 | tf_op jit(solution)/shard_map/ppermute | solution.py:15
  10.2 5.6 %collective-permute-start.1 = (f32[2,128,512]{2,1,0:T(8,128)}, f32[2,128,512]{2,1,0:T(8,128)S(1)}, u32[]{:S(2)}, u32[]{:S(2)}) collective-permute-start(f32[2,128,512]{2,1,0:T(8,128)} %param.10), channel_id=1, source_target_pairs={{8,0},{16,8},{24,16},{32,24},{40,32},{48,40},{56,48},{64,56},{72,6... | collective-permute-start | bytes 1572872 | tf_op jit(solution)/shard_map/ppermute | solution.py:16
  15.8 1.9 add_bitcast_fusion
  17.7 4.8 %collective-permute-done = f32[2,128,512]{2,1,0:T(8,128)S(1)} collective-permute-done((f32[2,128,512]{2,1,0:T(8,128)}, f32[2,128,512]{2,1,0:T(8,128)S(1)}, u32[]{:S(2)}, u32[]{:S(2)}) %collective-permute-start) | collective-permute-done | bytes 524320 | tf_op jit(solution)/shard_map/ppermute | solution.py:15
  22.4 3.2 collective-permute-done.1
  26.8 60.4 %while.33 = (s32[]{:T(128)}, bf16[3,1,256,256]{3,2,1,0:T(8,128)(2,1)}, bf16[3,1,256,256]{3,2,1,0:T(8,128)(2,1)}, f32[3,1,256,256]{3,2,1,0:T(8,128)}, f32[3,1,256...) while((s32[]{:T(128)}, ...), condition=%wide.region_1.2_spmd.clone.clone, body=%wide.region_0.1_spmd.clone.clone.sunk | while | flops 278003712 | bytes 5506879 | solution.py:71
  34.4 2.0 bitcast_dynamic-update-slice_fusion.3
  42.1 1.9 fusion.199
  45.2 1.9 fusion.197
  54.6 2.0 bitcast_dynamic-update-slice_fusion.3
  62.3 1.9 fusion.199
  65.3 1.9 fusion.197
  74.7 2.0 bitcast_dynamic-update-slice_fusion.3
  85.4 1.9 fusion.197
  87.3 2.4 multiply_add_fusion
  90.0 54.6 %all-gather.3.cloned.1.call-done = f32[24,1,256,256]{3,2,1,0:T(8,128)} async-done(((f32[3,1,256,256]{3,2,1,0:T(8,128)}), f32[24,1,256,256]{3,2,1,0:T(8,128)}) %all-gather.3.cloned.1.call-update) | async-done | bytes 6291472 | tf_op jit(solution)/shard_map/all_gather | solution.py:73
  144.6 3.4 %bitcast_reduce_fusion = f32[3,256,256]{2,1,0:T(8,128)S(1)} fusion(f32[8,3,256,256]{3,2,1,0:T(8,128)} %bitcast.195), kind=kLoop, calls=%fused_computation.160 | loop fusion | flops 1376256 | bytes 7077888 | tf_op jit(solution)/shard_map/reduce_sum | solution.py:74
  149.6 96.3 %while.34 = (s32[]{:T(128)}, f32[3,384,512]{2,1,0:T(8,128)S(1)}, s32[3]{0:T(128)S(1)}, s32[3]{0:T(128)S(1)}, s32[]{:T(128)}, /*index=5*/f32[1,256,256]{2,1,0:T(8...) while((s32[]{:T(128)}, f32[3,384,512]{2,1,0:T(8,128)S(1)}, ...), condition=%wide.region_4.5_spmd.clone.clone, body=%wide.region_3.4_spmd.clone.clone.sunk | while | flops 279183360 | bytes 10223899 | solution.py:106
  156.5 2.1 fusion.214
  159.7 3.1 fusion.216
  169.3 13.6 %dynamic_update_slice.42 = f32[3,384,512]{2,1,0:T(8,128)S(1)} dynamic-update-slice(f32[3,384,512]{2,1,0:T(8,128)S(1)} %get-tuple-element.786, f32[3,256,256]{2,1,0:T(8,128)S(1)} %fusion.217, s32[]{:T(128)} %constant.88.clone.1..sunk.1, s32[]{:T(128)S(6)} %select_n.210, s32[]{:T(128)S(6)} %select_n.211) | dynamic-update-slice | bytes 1572868 | tf_op jit(solution)/shard_map/while/body/eval_jaxpr/dynamic_update_slice | solution.py:104
  189.8 2.1 fusion.214
  193.1 3.1 fusion.216
  202.6 11.0 %dynamic_update_slice.42 = f32[3,384,512]{2,1,0:T(8,128)S(1)} dynamic-update-slice(f32[3,384,512]{2,1,0:T(8,128)S(1)} %get-tuple-element.786, f32[3,256,256]{2,1,0:T(8,128)S(1)} %fusion.217, s32[]{:T(128)} %constant.88.clone.1..sunk.1, s32[]{:T(128)S(6)} %select_n.210, s32[]{:T(128)S(6)} %select_n.211) | dynamic-update-slice | bytes 1572868 | tf_op jit(solution)/shard_map/while/body/eval_jaxpr/dynamic_update_slice | solution.py:104
  220.6 2.1 fusion.214
  223.8 3.1 fusion.216
  233.4 12.6 %dynamic_update_slice.42 = f32[3,384,512]{2,1,0:T(8,128)S(1)} dynamic-update-slice(f32[3,384,512]{2,1,0:T(8,128)S(1)} %get-tuple-element.786, f32[3,256,256]{2,1,0:T(8,128)S(1)} %fusion.217, s32[]{:T(128)} %constant.88.clone.1..sunk.1, s32[]{:T(128)S(6)} %select_n.210, s32[]{:T(128)S(6)} %select_n.211) | dynamic-update-slice | bytes 1572868 | tf_op jit(solution)/shard_map/while/body/eval_jaxpr/dynamic_update_slice | solution.py:104
  246.2 1.9 collective-permute-start.2
  248.1 4.0 %collective-permute-start.3 = (f32[3,128,512]{2,1,0:T(8,128)S(1)}, f32[3,128,512]{2,1,0:T(8,128)S(1)}, u32[]{:S(2)}, u32[]{:S(2)}) collective-permute-start(f32[3,128,512]{2,1,0:T(8,128)S(1)} %get-tuple-element.551), channel_id=1, source_target_pairs={{8,0},{16,8},{24,16},{32,24},{40,32},{48,40},{56,48},{64,56},{72,6... | collective-permute-start | bytes 2359304 | tf_op jit(solution)/shard_map/ppermute | solution.py:16
  252.1 15.7 %collective-permute-done.2 = f32[3,128,512]{2,1,0:T(8,128)S(1)} collective-permute-done((f32[3,128,512]{2,1,0:T(8,128)S(1)}, f32[3,128,512]{2,1,0:T(8,128)S(1)}, u32[]{:S(2)}, u32[]{:S(2)}) %collective-permute-start.2) | collective-permute-done | bytes 786464 | tf_op jit(solution)/shard_map/ppermute | solution.py:15
  267.8 3.9 %collective-permute-done.3 = f32[3,128,512]{2,1,0:T(8,128)S(1)} collective-permute-done((f32[3,128,512]{2,1,0:T(8,128)S(1)}, f32[3,128,512]{2,1,0:T(8,128)S(1)}, u32[]{:S(2)}, u32[]{:S(2)}) %collective-permute-start.3) | collective-permute-done | bytes 786464 | tf_op jit(solution)/shard_map/ppermute | solution.py:16
  272.9 39.9 %reduce-scatter.2.cloned.1.call-done = f32[3,16,512]{2,1,0:T(8,128)} async-done(((f32[3,128,512]{2,1,0:T(8,128)}), f32[3,16,512]{2,1,0:T(8,128)}) %reduce-scatter.2.cloned.1.call-update) | async-done | bytes 98320 | tf_op jit(solution)/shard_map/reduce_scatter | solution.py:116
  (80 shorter events, 65.9 us)
Async XLA Ops:
  6.5 20.3 %copy-start.1 = (s32[3]{0:T(128)S(1)}, s32[3]{0:T(128)}, u32[]{:S(2)}) copy-start(s32[3]{0:T(128)} %param.13) | copy-start | bytes 40
  6.5 20.3 %copy-start.2 = (s32[3]{0:T(128)S(1)}, s32[3]{0:T(128)}, u32[]{:S(2)}) copy-start(s32[3]{0:T(128)} %param.14) | copy-start | bytes 40
  6.5 138.1 %all-gather.3.cloned.1.call-start = ((), (), s32[]{:S(2)}) async-start(), calls=%async_computation.2 | async-start | bytes 7077888 | tf_op jit(solution)/shard_map/all_gather | solution.py:73
  6.5 15.9 %collective-permute-start = (f32[2,128,512]{2,1,0:T(8,128)}, f32[2,128,512]{2,1,0:T(8,128)S(1)}, u32[]{:S(2)}, u32[]{:S(2)}) collective-permute-start(f32[2,128,512]{2,1,0:T(8,128)} %param.10), channel_id=1, source_target_pairs={{0,8},{8,16},{16,24},{24,32},{32,40},{40,48},{48,56},{56,64},{64,7... | collective-permute-start | bytes 1572872 | tf_op jit(solution)/shard_map/ppermute | solution.py:15
  10.2 15.5 %collective-permute-start.1 = (f32[2,128,512]{2,1,0:T(8,128)}, f32[2,128,512]{2,1,0:T(8,128)S(1)}, u32[]{:S(2)}, u32[]{:S(2)}) collective-permute-start(f32[2,128,512]{2,1,0:T(8,128)} %param.10), channel_id=1, source_target_pairs={{8,0},{16,8},{24,16},{32,24},{40,32},{48,40},{56,48},{64,56},{72,6... | collective-permute-start | bytes 1572872 | tf_op jit(solution)/shard_map/ppermute | solution.py:16
  89.7 223.1 %reduce-scatter.2.cloned.1.call-start = ((), (), s32[]{:S(2)}) async-start(), calls=%async_computation.1 | async-start | bytes 884736 | tf_op jit(solution)/shard_map/reduce_scatter | solution.py:116
  144.6 3.4 %copy-start = (f32[3,256,256]{2,1,0:T(8,128)S(1)}, f32[3,256,256]{2,1,0:T(8,128)}, u32[]{:S(2)}) copy-start(f32[3,256,256]{2,1,0:T(8,128)} %param.12) | copy-start | bytes 2359300
  246.2 21.6 %collective-permute-start.2 = (f32[3,128,512]{2,1,0:T(8,128)S(1)}, f32[3,128,512]{2,1,0:T(8,128)S(1)}, u32[]{:S(2)}, u32[]{:S(2)}) collective-permute-start(f32[3,128,512]{2,1,0:T(8,128)S(1)} %get-tuple-element.550), channel_id=1, source_target_pairs={{0,8},{8,16},{16,24},{24,32},{32,40},{40,48},{48,56},{56,64},{64,7... | collective-permute-start | bytes 2359304 | tf_op jit(solution)/shard_map/ppermute | solution.py:15
  248.1 23.6 %collective-permute-start.3 = (f32[3,128,512]{2,1,0:T(8,128)S(1)}, f32[3,128,512]{2,1,0:T(8,128)S(1)}, u32[]{:S(2)}, u32[]{:S(2)}) collective-permute-start(f32[3,128,512]{2,1,0:T(8,128)S(1)} %get-tuple-element.551), channel_id=1, source_target_pairs={{8,0},{16,8},{24,16},{32,24},{40,32},{48,40},{56,48},{64,56},{72,6... | collective-permute-start | bytes 2359304 | tf_op jit(solution)/shard_map/ppermute | solution.py:16
Sparse Core Ops, SparseCore 0:
  89.9 54.6 all-gather.2
  273.0 39.7 reduce-scatter.1
